TPU v7x, 32 devices: a whole 2x2x4 slice. The times are simulated.
32 devices in a mesh: space: 4 (over z), dp: 8 (over y, x, core).
Axes of the slice: x: 2, y: 2, z: 4, core: 2. Of those that a mesh axis runs over, the one named last changes fastest.
Arguments:
- features: bfloat16 [8, 12, 128, 320], P('dp', 'space'), may hold values from -6 to 6
- cotangent: bfloat16 [8, 12, 128, 320], P('dp', 'space'), may hold values from -6 to 6
- norm_gain: float32 [320], replicated, may hold values from 0.1 to 1.9
- norm_bias: float32 [320], replicated, may hold values from -0.5 to 0.5
- weight: bfloat16 [2880, 320], P('dp'), may hold values from -0.109375 to 0.109375
- moment_one: float32 [2880, 320], P('dp'), may hold values from -332.55374 to 332.55374
- moment_two: float32 [2880, 320], P('dp'), may hold values from 768 to 6144
- heights: int32 [8], P('dp'), may hold values from 6 to 12, as said below
- widths: int32 [8], P('dp'), may hold values from 64 to 128, as said below
Outputs:
- block_out: bfloat16 [8, 12, 128, 320], P('dp', 'space')
- input_grad: bfloat16 [8, 12, 128, 320], P('dp', 'space')
- weight_grad: float32 [2880, 320], P('dp')
- adam_update: float32 [2880, 320], P('dp')
Inputs may be any that keep to these rules, and one draw needn't show every extreme that they name: Image i occupies canvas rows 0 to heights[i] - 1; some image has all 12 rows. Image i occupies canvas columns 0 to widths[i] - 1; some image has all 128 columns.
All inputs are finite; a program needn't handle non-finite values.
Results may differ from a plain program's by a relative error of at most 0.017.
Values may be sent and summed in bfloat16 or wider, within the bound.
No kernel may reach another device: no remote copies, remote signals or barrier semaphores. Data moves between devices by JAX's collectives and lax.ppermute only.
A program may use at most 64 MiB of HBM per device.

v0:
```python
import jax
import jax.numpy as jnp
from jax import lax
from jax.sharding import PartitionSpec as P

GROUPS = 32


def with_halo(cells, sides, width):
    for axis, dim in sides:
        count = lax.axis_size(axis)
        ends = count - 1
        head = lax.slice_in_dim(cells, 0, width, axis=dim)
        tail = lax.slice_in_dim(cells, cells.shape[dim] - width, cells.shape[dim], axis=dim)
        cells = jnp.concatenate(
            [
                lax.ppermute(tail, axis, [(i, (i + 1) % count) for i in range(ends)]),
                cells,
                lax.ppermute(head, axis, [((i + 1) % count, i) for i in range(ends)]),
            ],
            axis=dim,
        )
    return cells


def space_sum(parts, axis):
    count = lax.axis_size(axis)
    if count & count - 1:
        return lax.psum(parts, axis)
    step = 1
    while step < count:
        pairs = [(i, i ^ step) for i in range(count)]
        parts = tuple((p + q for p, q in zip(parts, lax.ppermute(parts, axis, pairs))))
        step *= 2
    return parts


def group_sum(values, groups):
    height_dev, width_dev, channels = values.shape
    return values.reshape(height_dev, width_dev, groups, channels // groups).sum(axis=(0, 1, 3))


def spread_groups(statistic, channels):
    return jnp.repeat(statistic, channels // statistic.shape[0])


def pad_columns(padded_rows):
    return jnp.pad(padded_rows, ((0, 0), (1, 1), (0, 0)))


def local(
    features, cotangent, norm_gain, norm_bias, weight, moment_one, moment_two, heights, widths
):
    latent = features[0]
    height_dev, width_dev, channels = latent.shape
    row_ids = lax.axis_index("space") * height_dev + jnp.arange(height_dev, dtype=jnp.int32)
    inside = (
        (row_ids < heights[0])[:, None]
        & (jnp.arange(width_dev, dtype=jnp.int32) < widths[0])[None, :]
    ).astype(jnp.float32)[..., None]
    cell_count = (heights[0] * widths[0] * (channels // GROUPS)).astype(jnp.float32)
    gathered = lax.all_gather(weight, "dp", axis=0, tiled=True)
    tap_weights = gathered.reshape(9, channels, channels)
    values = latent.astype(jnp.float32) * inside
    group_total, squares = space_sum(
        (group_sum(values, GROUPS), group_sum(values * values, GROUPS)), "space"
    )
    center = group_total / cell_count
    spread = squares / cell_count - center * center
    inverse = lax.rsqrt(spread + 1e-05)
    normed = (values - spread_groups(center, channels)) * spread_groups(inverse, channels) * inside
    before = normed * norm_gain + norm_bias
    activated = (jax.nn.silu(before) * inside).astype(jnp.bfloat16)
    act_pad = pad_columns(with_halo(activated, (("space", 0),), 1))
    output = jnp.zeros((height_dev * width_dev, channels), jnp.float32)
    for row_off in range(3):
        for col_off in range(3):
            window = act_pad[row_off : row_off + height_dev, col_off : col_off + width_dev].reshape(
                -1, channels
            )
            output = output + jnp.dot(
                window, tap_weights[row_off * 3 + col_off], preferred_element_type=jnp.float32
            )
    block_out = (output.reshape(height_dev, width_dev, channels) * inside).astype(jnp.bfloat16)
    masked = cotangent[0] * inside.astype(jnp.bfloat16)
    cot_pad = pad_columns(with_halo(masked, (("space", 0),), 1))
    flat_cot = masked.reshape(-1, channels)
    upstream = jnp.zeros((height_dev * width_dev, channels), jnp.float32)
    tap_grads = []
    for row_off in range(3):
        for col_off in range(3):
            tap_index = row_off * 3 + col_off
            window = act_pad[row_off : row_off + height_dev, col_off : col_off + width_dev].reshape(
                -1, channels
            )
            tap_grads.append(
                lax.dot_general(
                    window, flat_cot, (((0,), (0,)), ((), ())), preferred_element_type=jnp.float32
                )
            )
            cot_window = cot_pad[
                2 - row_off : 2 - row_off + height_dev, 2 - col_off : 2 - col_off + width_dev
            ].reshape(-1, channels)
            upstream = upstream + lax.dot_general(
                cot_window,
                tap_weights[tap_index],
                (((1,), (1,)), ((), ())),
                preferred_element_type=jnp.float32,
            )
    weight_terms = jnp.stack(tap_grads).reshape(9 * channels, channels)
    gate_sig = jax.nn.sigmoid(before)
    silu_slope = gate_sig * (1.0 + before * (1.0 - gate_sig))
    scaled = upstream.reshape(height_dev, width_dev, channels) * silu_slope * inside * norm_gain
    local_first = group_sum(scaled, GROUPS)
    local_second = group_sum(scaled * normed, GROUPS)
    dp_size = lax.axis_size("dp")
    grad_piece = lax.psum_scatter(
        weight_terms.astype(jnp.bfloat16).reshape(dp_size, -1, channels),
        "dp",
        scatter_dimension=0,
        tiled=False,
    )
    sum_first, sum_second = space_sum((local_first, local_second), "space")
    grad_piece = lax.psum(grad_piece, "space").astype(jnp.float32)
    first = sum_first / cell_count
    second = sum_second / cell_count
    input_grad = (
        spread_groups(inverse, channels)
        * (scaled - spread_groups(first, channels) - normed * spread_groups(second, channels))
        * inside
    ).astype(jnp.bfloat16)
    first_new = 0.9 * moment_one + 0.1 * grad_piece
    second_new = 0.999 * moment_two + 0.001 * grad_piece * grad_piece
    adam_update = first_new / (1.0 - 0.9**10) / (jnp.sqrt(second_new / (1.0 - 0.999**10)) + 1e-08)
    return (block_out[None], input_grad[None], grad_piece, adam_update)


def solution(mesh):
    placed = (
        P("dp", "space", None, None),
        P("dp", "space", None, None),
        P(),
        P(),
        P("dp", None),
        P("dp", None),
        P("dp", None),
        P("dp"),
        P("dp"),
    )
    return jax.shard_map(
        local,
        mesh=mesh,
        in_specs=placed,
        out_specs=(
            P("dp", "space", None, None),
            P("dp", "space", None, None),
            P("dp", None),
            P("dp", None),
        ),
        check_vma=False,
    )
```

profile of v0, /device:TPU:0, one launch (start us, length us, event | category | flops | bytes accessed | tf_op | source)
XLA Modules:
  0.0 191.6 jit_solution(13779045567825138440)
XLA Ops:
  8.6 1.1 multiply_reduce_fusion.1
  10.0 3.1 %collective-permute-start = (f32[32]{0:T(128)S(1)}, f32[32]{0:T(128)S(1)}, u32[]{:S(2)}, u32[]{:S(2)}) collective-permute-start(f32[32]{0:T(128)S(1)} %reduce_sum.51), channel_id=1, source_target_pairs={{0,8},{8,0},{16,24},{24,16},{1,9},{9,1},{17,25},{25,17},{2,10},{10... | collective-permute-start | bytes 392 | tf_op jit(solution)/shard_map/ppermute | solution.py:33
  13.4 1.2 collective-permute-done
  14.6 3.0 %collective-permute-start.1 = (f32[32]{0:T(128)S(1)}, f32[32]{0:T(128)S(1)}, u32[]{:S(2)}, u32[]{:S(2)}) collective-permute-start(f32[32]{0:T(128)S(1)} %add.163), channel_id=1, source_target_pairs={{0,16},{8,24},{16,0},{24,8},{1,17},{9,25},{17,1},{25,9},{2,18},{10... | collective-permute-start | bytes 392 | tf_op jit(solution)/shard_map/ppermute | solution.py:33
  17.6 1.9 collective-permute-start.3
  19.5 2.6 %collective-permute-done.3 = f32[32]{0:T(128)S(1)} collective-permute-done((f32[32]{0:T(128)S(1)}, f32[32]{0:T(128)S(1)}, u32[]{:S(2)}, u32[]{:S(2)}) %collective-permute-start.3) | collective-permute-done | bytes 160 | tf_op jit(solution)/shard_map/ppermute | solution.py:33
  22.5 1.3 multiply_convert_fusion.4
  23.7 3.5 %collective-permute-start.4 = (bf16[1,128,320]{1,2,0:T(8,128)(2,1)S(1)}, bf16[1,128,320]{1,2,0:T(8,128)(2,1)S(1)}, u32[]{:S(2)}, u32[]{:S(2)}) collective-permute-start(bf16[1,128,320]{1,2,0:T(8,128)(2,1)S(1)} %get-tuple-element.30), channel_id=1, source_target_pairs={{0,8},{8,16},{16,24},{1,9},{9,17},{17,25},{2,10},{10,18},{18,26},{... | collective-permute-start | bytes 245768 | tf_op jit(solution)/shard_map/ppermute | solution.py:17
  27.2 1.3 collective-permute-start.5
  28.5 1.0 bitcast_multiply_fusion.2
  29.5 4.1 %collective-permute-done.5 = bf16[1,128,320]{1,2,0:T(8,128)(2,1)S(1)} collective-permute-done((bf16[1,128,320]{1,2,0:T(8,128)(2,1)S(1)}, bf16[1,128,320]{1,2,0:T(8,128)(2,1)S(1)}, u32[]{:S(2)}, u32[]{:S(2)}) %collective-permute-start.5) | collective-permute-done | bytes 81952 | tf_op jit(solution)/shard_map/ppermute | solution.py:19
  34.0 1.0 fusion.29
  35.0 1.0 fusion.15
  36.0 1.1 fusion.27
  37.1 1.0 fusion.25
  38.1 1.2 fusion.23
  39.4 1.1 fusion.21
  40.4 1.0 fusion.19
  41.4 1.1 fusion.13
  42.5 1.1 fusion.17
  43.6 4.2 %copy.68 = bf16[8,360,320]{1,2,0:T(8,128)(2,1)} copy(bf16[8,360,320]{2,1,0:T(8,128)(2,1)} %bitcast.48) | data formatting | bytes 3686400 | tf_op jit(solution)/shard_map/convert_element_type | solution.py:118
  47.8 38.9 %reduce-scatter.2.cloned.1.call-done = bf16[1,360,320]{1,2,0:T(8,128)(2,1)} async-done(((bf16[8,360,320]{1,2,0:T(8,128)(2,1)}), bf16[1,360,320]{1,2,0:T(8,128)(2,1)}) %reduce-scatter.2.cloned.1.call-update) | async-done | bytes 230416 | tf_op jit(solution)/shard_map/reduce_scatter | solution.py:117
  86.8 0.7 all-gather.3.cloned.1.call-update
  87.5 3.4 %collective-permute-start.6 = (bf16[1,128,320]{1,2,0:T(8,128)(2,1)S(1)}, bf16[1,128,320]{1,2,0:T(8,128)(2,1)S(1)}, u32[]{:S(2)}, u32[]{:S(2)}) collective-permute-start(bf16[1,128,320]{1,2,0:T(8,128)(2,1)S(1)} %get-tuple-element.26), channel_id=1, source_target_pairs={{0,8},{8,16},{16,24},{1,9},{9,17},{17,25},{2,10},{10,18},{18,26},{... | collective-permute-start | bytes 245768 | tf_op jit(solution)/shard_map/ppermute | solution.py:17
  90.9 1.3 collective-permute-start.7
  92.8 1.0 copy.49
  93.8 4.8 %collective-permute-done.7 = bf16[1,128,320]{1,2,0:T(8,128)(2,1)S(1)} collective-permute-done((bf16[1,128,320]{1,2,0:T(8,128)(2,1)S(1)}, bf16[1,128,320]{1,2,0:T(8,128)(2,1)S(1)}, u32[]{:S(2)}, u32[]{:S(2)}) %collective-permute-start.7) | collective-permute-done | bytes 81952 | tf_op jit(solution)/shard_map/ppermute | solution.py:19
  98.7 0.6 copy-done.15
  100.0 0.9 copy.56
  100.9 1.7 pad_maximum_fusion
  102.6 1.8 copy.57
  104.4 0.9 copy.58
  105.3 0.9 copy.59
  106.3 0.9 copy.61
  107.2 0.9 copy.62
  108.1 0.9 copy.63
  109.0 0.9 copy.64
  109.9 1.0 fusion.102
  110.9 1.2 copy.43
  112.1 0.9 copy.45
  113.0 0.9 copy.46
  113.9 0.9 copy.47
  114.8 0.9 copy.51
  115.7 0.9 copy.50
  117.1 7.1 %all-reduce.4.cloned.1.call-done = bf16[360,320]{0,1:T(8,128)(2,1)} async-done(((bf16[360,320]{0,1:T(8,128)(2,1)}), bf16[360,320]{0,1:T(8,128)(2,1)}) %all-reduce.4.cloned.1.call-update) | async-done | bytes 230416 | tf_op jit(solution)/shard_map/psum | solution.py:124
  124.2 2.3 %fusion.35 = (f32[360,320]{0,1:T(8,128)}, f32[360,320]{0,1:T(8,128)}) fusion(f32[360,320]{0,1:T(8,128)S(1)} %copy-done.11, f32[360,320]{0,1:T(8,128)} %param.14, bf16[360,320]{0,1:T(8,128)(2,1)} %all-reduce.4.cloned.1.call-done), kind=kLoop, calls=%fused_computation.65 | loop fusion | flops 1382400 | bytes 2073600 | tf_op jit(solution)/shard_map/div | solution.py:134
  126.5 27.0 %all-gather.3.cloned.1.call-done = bf16[8,360,320]{1,2,0:T(8,128)(2,1)} async-done(((bf16[1,360,320]{1,2,0:T(8,128)(2,1)}), bf16[8,360,320]{1,2,0:T(8,128)(2,1)}) %all-gather.3.cloned.1.call-update) | async-done | bytes 1843216 | tf_op jit(solution)/shard_map/all_gather | solution.py:62
  153.5 4.0 %copy.44 = bf16[8,360,320]{1,0,2:T(8,128)(2,1)} copy(bf16[8,360,320]{1,2,0:T(8,128)(2,1)} %all-gather.3.cloned.1.call-done) | data formatting | bytes 3686400 | tf_op jit(solution)/shard_map/all_gather | solution.py:62
  157.4 3.4 %reshape.284 = bf16[2880,320]{0,1:T(8,128)(2,1)S(1)} reshape(bf16[8,360,320]{1,0,2:T(8,128)(2,1)} %copy.44) | data formatting | bytes 3686400
  161.2 1.3 fusion.68
  164.3 0.5 fusion.2
  166.1 1.4 fusion.81
  167.5 1.5 convolution_add_fusion.8
  169.4 0.5 convolution_add_fusion.6
  170.4 0.5 convolution_add_fusion.4
  171.3 0.5 convolution_add_fusion.2
  172.0 0.7 fusion.100
  173.0 1.6 collective-permute-start.8
  174.7 0.6 collective-permute-start.10
  175.6 1.0 collective-permute-done.8
  176.6 2.4 %collective-permute-start.9 = (f32[32]{0:T(128)S(1)}, f32[32]{0:T(128)S(1)}, u32[]{:S(2)}, u32[]{:S(2)}) collective-permute-start(f32[32]{0:T(128)S(1)} %add.198), channel_id=1, source_target_pairs={{0,16},{8,24},{16,0},{24,8},{1,17},{9,25},{17,1},{25,9},{2,18},{10... | collective-permute-start | bytes 392 | tf_op jit(solution)/shard_map/ppermute | solution.py:33
  179.0 1.8 collective-permute-start.11
  181.0 2.4 %collective-permute-done.11 = f32[32]{0:T(128)S(1)} collective-permute-done((f32[32]{0:T(128)S(1)}, f32[32]{0:T(128)S(1)}, u32[]{:S(2)}, u32[]{:S(2)}) %collective-permute-start.11) | collective-permute-done | bytes 160 | tf_op jit(solution)/shard_map/ppermute | solution.py:33
  183.8 1.3 multiply_convert_fusion.1
  (100 shorter events, 9.2 us)
Async XLA Ops:
  7.2 79.6 %reduce-scatter.2.cloned.1.call-start = ((), (), s32[]{:S(2)}) async-start(), calls=%async_computation.1 | async-start | bytes 2211840 | tf_op jit(solution)/shard_map/reduce_scatter | solution.py:117
  10.0 4.6 %collective-permute-start = (f32[32]{0:T(128)S(1)}, f32[32]{0:T(128)S(1)}, u32[]{:S(2)}, u32[]{:S(2)}) collective-permute-start(f32[32]{0:T(128)S(1)} %reduce_sum.51), channel_id=1, source_target_pairs={{0,8},{8,0},{16,24},{24,16},{1,9},{9,1},{17,25},{25,17},{2,10},{10... | collective-permute-start | bytes 392 | tf_op jit(solution)/shard_map/ppermute | solution.py:33
  13.3 4.3 %collective-permute-start.2 = (f32[32]{0:T(128)S(1)}, f32[32]{0:T(128)S(1)}, u32[]{:S(2)}, u32[]{:S(2)}) collective-permute-start(f32[32]{0:T(128)S(1)} %reduce_sum.54), channel_id=1, source_target_pairs={{0,8},{8,0},{16,24},{24,16},{1,9},{9,1},{17,25},{25,17},{2,10},{10... | collective-permute-start | bytes 392 | tf_op jit(solution)/shard_map/ppermute | solution.py:33
  14.6 4.9 %collective-permute-start.1 = (f32[32]{0:T(128)S(1)}, f32[32]{0:T(128)S(1)}, u32[]{:S(2)}, u32[]{:S(2)}) collective-permute-start(f32[32]{0:T(128)S(1)} %add.163), channel_id=1, source_target_pairs={{0,16},{8,24},{16,0},{24,8},{1,17},{9,25},{17,1},{25,9},{2,18},{10... | collective-permute-start | bytes 392 | tf_op jit(solution)/shard_map/ppermute | solution.py:33
  17.6 4.4 %collective-permute-start.3 = (f32[32]{0:T(128)S(1)}, f32[32]{0:T(128)S(1)}, u32[]{:S(2)}, u32[]{:S(2)}) collective-permute-start(f32[32]{0:T(128)S(1)} %add.165), channel_id=1, source_target_pairs={{0,16},{8,24},{16,0},{24,8},{1,17},{9,25},{17,1},{25,9},{2,18},{10... | collective-permute-start | bytes 392 | tf_op jit(solution)/shard_map/ppermute | solution.py:33
  23.7 5.8 %collective-permute-start.4 = (bf16[1,128,320]{1,2,0:T(8,128)(2,1)S(1)}, bf16[1,128,320]{1,2,0:T(8,128)(2,1)S(1)}, u32[]{:S(2)}, u32[]{:S(2)}) collective-permute-start(bf16[1,128,320]{1,2,0:T(8,128)(2,1)S(1)} %get-tuple-element.30), channel_id=1, source_target_pairs={{0,8},{8,16},{16,24},{1,9},{9,17},{17,25},{2,10},{10,18},{18,26},{... | collective-permute-start | bytes 245768 | tf_op jit(solution)/shard_map/ppermute | solution.py:17
  27.2 6.3 %collective-permute-start.5 = (bf16[1,128,320]{1,2,0:T(8,128)(2,1)S(1)}, bf16[1,128,320]{1,2,0:T(8,128)(2,1)S(1)}, u32[]{:S(2)}, u32[]{:S(2)}) collective-permute-start(bf16[1,128,320]{1,2,0:T(8,128)(2,1)S(1)} %get-tuple-element.31), channel_id=1, source_target_pairs={{8,0},{16,8},{24,16},{9,1},{17,9},{25,17},{10,2},{18,10},{26,18},{... | collective-permute-start | bytes 245768 | tf_op jit(solution)/shard_map/ppermute | solution.py:19
  34.0 4.2 %copy-start = (bf16[1,3,128,320]{2,3,1,0:T(8,128)(2,1)S(1)}, bf16[1,3,128,320]{2,3,1,0:T(8,128)(2,1)}, u32[]{:S(2)}) copy-start(bf16[1,3,128,320]{2,3,1,0:T(8,128)(2,1)} %param.9) | copy-start | bytes 737284
  34.0 4.2 %copy-start.10 = (bf16[1,3,128,320]{2,3,1,0:T(8,128)(2,1)S(1)}, bf16[1,3,128,320]{2,3,1,0:T(8,128)(2,1)}, u32[]{:S(2)}) copy-start(bf16[1,3,128,320]{2,3,1,0:T(8,128)(2,1)} %param.10) | copy-start | bytes 737284
  34.0 4.1 %copy-start.17 = (f32[320]{0:T(512)S(1)}, f32[320]{0:T(512)}, u32[]{:S(2)}) copy-start(f32[320]{0:T(512)} %param.12) | copy-start | bytes 3844
  34.0 4.1 %copy-start.18 = (f32[320]{0:T(512)S(1)}, f32[320]{0:T(512)}, u32[]{:S(2)}) copy-start(f32[320]{0:T(512)} %param.11) | copy-start | bytes 3844
  47.8 76.4 %all-reduce.4.cloned.1.call-start = ((), (), s32[]{:S(2)}) async-start(), calls=%async_computation.2 | async-start | bytes 491520 | tf_op jit(solution)/shard_map/psum | solution.py:124
  86.8 66.7 %all-gather.3.cloned.1.call-start = ((), (), s32[]{:S(2)}) async-start(), calls=%async_computation.3 | async-start | bytes 2211840 | tf_op jit(solution)/shard_map/all_gather | solution.py:62
  87.5 6.3 %collective-permute-start.6 = (bf16[1,128,320]{1,2,0:T(8,128)(2,1)S(1)}, bf16[1,128,320]{1,2,0:T(8,128)(2,1)S(1)}, u32[]{:S(2)}, u32[]{:S(2)}) collective-permute-start(bf16[1,128,320]{1,2,0:T(8,128)(2,1)S(1)} %get-tuple-element.26), channel_id=1, source_target_pairs={{0,8},{8,16},{16,24},{1,9},{9,17},{17,25},{2,10},{10,18},{18,26},{... | collective-permute-start | bytes 245768 | tf_op jit(solution)/shard_map/ppermute | solution.py:17
  90.9 7.7 %collective-permute-start.7 = (bf16[1,128,320]{1,2,0:T(8,128)(2,1)S(1)}, bf16[1,128,320]{1,2,0:T(8,128)(2,1)S(1)}, u32[]{:S(2)}, u32[]{:S(2)}) collective-permute-start(bf16[1,128,320]{1,2,0:T(8,128)(2,1)S(1)} %get-tuple-element.27), channel_id=1, source_target_pairs={{8,0},{16,8},{24,16},{9,1},{17,9},{25,17},{10,2},{18,10},{26,18},{... | collective-permute-start | bytes 245768 | tf_op jit(solution)/shard_map/ppermute | solution.py:19
  93.8 4.8 %copy-start.14 = (bf16[1,128,320]{1,2,0:T(8,128)(2,1)}, bf16[1,128,320]{1,2,0:T(8,128)(2,1)S(1)}, u32[]{:S(2)}) copy-start(bf16[1,128,320]{1,2,0:T(8,128)(2,1)S(1)} %collective-permute-done.6) | copy-start | bytes 245764
  98.7 0.6 copy-start.15
  113.0 11.2 %copy-start.11 = (f32[360,320]{0,1:T(8,128)S(1)}, f32[360,320]{0,1:T(8,128)}, u32[]{:S(2)}) copy-start(f32[360,320]{0,1:T(8,128)} %param.15) | copy-start | bytes 1382404
  160.8 1.7 copy-start.9
  160.8 2.1 %copy-start.8 = (bf16[3,128,320]{2,1,0:T(8,128)(2,1)S(1)}, bf16[3,128,320]{2,1,0:T(8,128)(2,1)}, u32[]{:S(2)}) copy-start(bf16[3,128,320]{2,1,0:T(8,128)(2,1)} %copy.45) | copy-start | bytes 737284
  161.2 2.1 %copy-start.7 = (bf16[3,128,320]{2,1,0:T(8,128)(2,1)S(1)}, bf16[3,128,320]{2,1,0:T(8,128)(2,1)}, u32[]{:S(2)}) copy-start(bf16[3,128,320]{2,1,0:T(8,128)(2,1)} %copy.46) | copy-start | bytes 737284
  162.5 1.1 copy-start.6
  163.3 1.1 copy-start.12
  166.1 2.9 %copy-start.5 = (bf16[3,128,320]{2,1,0:T(8,128)(2,1)S(1)}, bf16[3,128,320]{2,1,0:T(8,128)(2,1)}, u32[]{:S(2)}) copy-start(bf16[3,128,320]{2,1,0:T(8,128)(2,1)} %copy.58) | copy-start | bytes 737284
  166.1 3.3 %copy-start.4 = (bf16[3,128,320]{2,1,0:T(8,128)(2,1)S(1)}, bf16[3,128,320]{2,1,0:T(8,128)(2,1)}, u32[]{:S(2)}) copy-start(bf16[3,128,320]{2,1,0:T(8,128)(2,1)} %copy.59) | copy-start | bytes 737284
  169.4 1.0 copy-start.3
  169.9 1.0 copy-start.1
  170.3 1.0 copy-start.2
  170.9 1.1 copy-start.13
  170.9 1.1 copy-start.16
  173.0 3.6 %collective-permute-start.8 = (f32[32]{0:T(128)S(1)}, f32[32]{0:T(128)S(1)}, u32[]{:S(2)}, u32[]{:S(2)}) collective-permute-start(f32[32]{0:T(128)S(1)} %reduce_sum.72), channel_id=1, source_target_pairs={{0,8},{8,0},{16,24},{24,16},{1,9},{9,1},{17,25},{25,17},{2,10},{10... | collective-permute-start | bytes 392 | tf_op jit(solution)/shard_map/ppermute | solution.py:33
  174.7 4.3 %collective-permute-start.10 = (f32[32]{0:T(128)S(1)}, f32[32]{0:T(128)S(1)}, u32[]{:S(2)}, u32[]{:S(2)}) collective-permute-start(f32[32]{0:T(128)S(1)} %reduce_sum.75), channel_id=1, source_target_pairs={{0,8},{8,0},{16,24},{24,16},{1,9},{9,1},{17,25},{25,17},{2,10},{10... | collective-permute-start | bytes 392 | tf_op jit(solution)/shard_map/ppermute | solution.py:33
  176.6 4.4 %collective-permute-start.9 = (f32[32]{0:T(128)S(1)}, f32[32]{0:T(128)S(1)}, u32[]{:S(2)}, u32[]{:S(2)}) collective-permute-start(f32[32]{0:T(128)S(1)} %add.198), channel_id=1, source_target_pairs={{0,16},{8,24},{16,0},{24,8},{1,17},{9,25},{17,1},{25,9},{2,18},{10... | collective-permute-start | bytes 392 | tf_op jit(solution)/shard_map/ppermute | solution.py:33
  179.0 4.4 %collective-permute-start.11 = (f32[32]{0:T(128)S(1)}, f32[32]{0:T(128)S(1)}, u32[]{:S(2)}, u32[]{:S(2)}) collective-permute-start(f32[32]{0:T(128)S(1)} %add.200), channel_id=1, source_target_pairs={{0,16},{8,24},{16,0},{24,8},{1,17},{9,25},{17,1},{25,9},{2,18},{10... | collective-permute-start | bytes 392 | tf_op jit(solution)/shard_map/ppermute | solution.py:33
Sparse Core Ops, SparseCore 0:
  47.9 38.8 reduce-scatter.1
  89.2 34.9 all-reduce.3
  126.1 27.3 all-gather.2
where the time goes:
time: 192 us
  waiting for transfers between devices  89.9 us (47%)
  local copies, waits for them, and re-layouts  31.8 us (17%)
  starting transfers between devices  24 us (12%)
  matrix products  20.2 us (11%)
  between operations  15.6 us (8%)
  other arithmetic  10.2 us (5%)
    reduce_scatter x1, waiting for transfers between devices, local(): lax.psum_scatter(weight_terms.astype(jnp.bfloat16).reshape(dp_size, -1, c...  38.9 us
    all_gather x1, waiting for transfers between devices, local(): gathered = lax.all_gather(weight, 'dp', axis=0, tiled=True)  27 us
    ppermute x8, starting transfers between devices, space_sum(): lax.ppermute(parts, axis, pairs)  14.4 us
    dot_general x9, matrix products, local(): lax.dot_general(window, flat_cot, (((0,), (0,)), ((), ())), preferred_ele...  9.52 us
    ppermute x2, waiting for transfers between devices, with_halo(): lax.ppermute(head, axis, [((i + 1) % count, i) for i in range(ends)])  8.87 us
    slice x9, local copies, waits for them, and re-layouts, local(): cot_pad[2 - row_off:2 - row_off + height_dev, 2 - col_off:2 - col_off + w...  8.5 us
    ppermute x8, waiting for transfers between devices, space_sum(): lax.ppermute(parts, axis, pairs)  7.28 us
    slice x9, local copies, waits for them, and re-layouts, local(): act_pad[row_off:row_off + height_dev, col_off:col_off + width_dev]  7.13 us
  transfers between devices with their start and end apart: 15, of which 9 were waited for; matrix products, arithmetic and copies ran while one was open for 12% of the time, Pallas kernels for 0%

commit v1 on v0

--- a/solution.py
+++ b/solution.py
@@ -121,7 +121,7 @@
         tiled=False,
     )
     sum_first, sum_second = space_sum((local_first, local_second), "space")
-    grad_piece = lax.psum(grad_piece, "space").astype(jnp.float32)
+    grad_piece = jnp.sum(lax.all_gather(grad_piece, "space"), axis=0).astype(jnp.float32)
     first = sum_first / cell_count
     second = sum_second / cell_count
     input_grad = (

time: 192 us -> 156 us (0.81)
  waiting for transfers between devices: 89.9 us -> 18.5 us
  blocking collectives: 0 us -> 22.2 us
  local copies, waits for them, and re-layouts: 31.8 us -> 42 us
    reduce_scatter x1, waiting for transfers between devices: 38.9 us -> 0.38 us  [local(): lax.psum_scatter(weight_terms.astype(jnp.bfloat16).reshape(dp_size, -1, c...]
    all_gather x1, waiting for transfers between devices: 27 us -> 4.44 us  [local(): gathered = lax.all_gather(weight, 'dp', axis=0, tiled=True)]
    all_gather x0 -> x1, blocking collectives: none -> 22.2 us  [local(): lax.all_gather(grad_piece, 'space')]
    psum x1 -> x0, waiting for transfers between devices: 7.13 us -> none  [local(): grad_piece = lax.psum(grad_piece, 'space').astype(jnp.float32)]
    slice x9, local copies, waits for them, and re-layouts: 8.5 us -> 13.2 us  [local(): cot_pad[2 - row_off:2 - row_off + height_dev, 2 - col_off:2 - col_off + w...]
    ppermute x2, waiting for transfers between devices: 8.87 us -> 5.66 us  [with_halo(): lax.ppermute(head, axis, [((i + 1) % count, i) for i in range(ends)])]
    unnamed x40 -> x75, local copies, waits for them, and re-layouts: 4.78 us -> 7.78 us
    slice x9, local copies, waits for them, and re-layouts: 7.13 us -> 9.11 us  [local(): act_pad[row_off:row_off + height_dev, col_off:col_off + width_dev]]
  transfers between devices with their start and end apart: 15 -> 14, of which waited for: 9 -> 8; matrix products, arithmetic and copies ran while one was open for 12% -> 23% of each run, Pallas kernels for 0% -> 0%
where the time goes in v1:
time: 156 us; the launch traced here: 155 us
  local copies, waits for them, and re-layouts  42 us (27%)
  starting transfers between devices  23.9 us (15%)
  blocking collectives  22.2 us (14%)
  matrix products  20.2 us (13%)
  waiting for transfers between devices  18.5 us (12%)
  between operations  16 us (10%)
  other arithmetic  11.8 us (8%)
    all_gather x1, blocking collectives, local(): lax.all_gather(grad_piece, 'space')  22.2 us
    ppermute x8, starting transfers between devices, space_sum(): lax.ppermute(parts, axis, pairs)  14.4 us
    slice x9, local copies, waits for them, and re-layouts, local(): cot_pad[2 - row_off:2 - row_off + height_dev, 2 - col_off:2 - col_off + w...  13.2 us
    dot_general x9, matrix products, local(): lax.dot_general(window, flat_cot, (((0,), (0,)), ((), ())), preferred_ele...  9.52 us
    slice x9, local copies, waits for them, and re-layouts, local(): act_pad[row_off:row_off + height_dev, col_off:col_off + width_dev]  9.11 us
    unnamed x75, local copies, waits for them, and re-layouts  7.78 us
    ppermute x8, waiting for transfers between devices, space_sum(): lax.ppermute(parts, axis, pairs)  7.28 us
    ppermute x2, starting transfers between devices, with_halo(): lax.ppermute(tail, axis, [(i, (i + 1) % count) for i in range(ends)])  6.86 us
  transfers between devices with their start and end apart: 14, of which 8 were waited for; matrix products, arithmetic and copies ran while one was open for 23% of the time, Pallas kernels for 0%

profile of v1, /device:TPU:0, one launch (start us, length us, event | category | flops | bytes accessed | tf_op | source)
XLA Modules:
  0.0 154.6 jit_solution(3051377698477733120)
XLA Ops:
  8.6 1.1 multiply_reduce_fusion.1
  10.0 3.1 %collective-permute-start = (f32[32]{0:T(128)S(1)}, f32[32]{0:T(128)S(1)}, u32[]{:S(2)}, u32[]{:S(2)}) collective-permute-start(f32[32]{0:T(128)S(1)} %reduce_sum.62), channel_id=1, source_target_pairs={{0,8},{8,0},{16,24},{24,16},{1,9},{9,1},{17,25},{25,17},{2,10},{10... | collective-permute-start | bytes 392 | tf_op jit(solution)/shard_map/ppermute | solution.py:33
  13.4 1.2 collective-permute-done
  14.6 3.0 %collective-permute-start.1 = (f32[32]{0:T(128)S(1)}, f32[32]{0:T(128)S(1)}, u32[]{:S(2)}, u32[]{:S(2)}) collective-permute-start(f32[32]{0:T(128)S(1)} %add.161), channel_id=1, source_target_pairs={{0,16},{8,24},{16,0},{24,8},{1,17},{9,25},{17,1},{25,9},{2,18},{10... | collective-permute-start | bytes 392 | tf_op jit(solution)/shard_map/ppermute | solution.py:33
  17.6 1.9 %collective-permute-start.3 = (f32[32]{0:T(128)S(1)}, f32[32]{0:T(128)S(1)}, u32[]{:S(2)}, u32[]{:S(2)}) collective-permute-start(f32[32]{0:T(128)S(1)} %add.163), channel_id=1, source_target_pairs={{0,16},{8,24},{16,0},{24,8},{1,17},{9,25},{17,1},{25,9},{2,18},{10... | collective-permute-start | bytes 392 | tf_op jit(solution)/shard_map/ppermute | solution.py:33
  19.5 2.6 %collective-permute-done.3 = f32[32]{0:T(128)S(1)} collective-permute-done((f32[32]{0:T(128)S(1)}, f32[32]{0:T(128)S(1)}, u32[]{:S(2)}, u32[]{:S(2)}) %collective-permute-start.3) | collective-permute-done | bytes 160 | tf_op jit(solution)/shard_map/ppermute | solution.py:33
  22.5 1.3 multiply_convert_fusion.4
  23.8 3.5 %collective-permute-start.4 = (bf16[1,128,320]{1,2,0:T(8,128)(2,1)S(1)}, bf16[1,128,320]{1,2,0:T(8,128)(2,1)S(1)}, u32[]{:S(2)}, u32[]{:S(2)}) collective-permute-start(bf16[1,128,320]{1,2,0:T(8,128)(2,1)S(1)} %get-tuple-element.32), channel_id=1, source_target_pairs={{0,8},{8,16},{16,24},{1,9},{9,17},{17,25},{2,10},{10,18},{18,26},{... | collective-permute-start | bytes 245768 | tf_op jit(solution)/shard_map/ppermute | solution.py:17
  27.2 1.3 collective-permute-start.5
  28.5 1.0 bitcast_multiply_fusion.2
  29.5 4.0 %collective-permute-done.5 = bf16[1,128,320]{1,2,0:T(8,128)(2,1)S(1)} collective-permute-done((bf16[1,128,320]{1,2,0:T(8,128)(2,1)S(1)}, bf16[1,128,320]{1,2,0:T(8,128)(2,1)S(1)}, u32[]{:S(2)}, u32[]{:S(2)}) %collective-permute-start.5) | collective-permute-done | bytes 81952 | tf_op jit(solution)/shard_map/ppermute | solution.py:19
  34.0 1.0 fusion.29
  35.0 1.0 fusion.15
  36.1 1.1 fusion.27
  37.1 1.0 fusion.25
  38.2 1.2 fusion.23
  39.4 1.1 fusion.21
  40.5 1.0 fusion.19
  41.5 1.0 fusion.13
  42.5 1.1 fusion.17
  43.6 4.1 %copy.66 = bf16[8,360,320]{1,2,0:T(8,128)(2,1)} copy(bf16[8,360,320]{2,1,0:T(8,128)(2,1)} %bitcast.48) | data formatting | bytes 3686400 | tf_op jit(solution)/shard_map/convert_element_type | solution.py:118
  47.8 0.7 all-gather.3.cloned.1.call-update
  48.5 0.7 fusion.103
  49.1 3.4 %collective-permute-start.6 = (bf16[1,128,320]{1,2,0:T(8,128)(2,1)}, bf16[1,128,320]{1,2,0:T(8,128)(2,1)}, u32[]{:S(2)}, u32[]{:S(2)}) collective-permute-start(bf16[1,128,320]{1,2,0:T(8,128)(2,1)} %get-tuple-element.28), channel_id=1, source_target_pairs={{0,8},{8,16},{16,24},{1,9},{9,17},{17,25},{2,10},{10,18},{18,26},{... | collective-permute-start | bytes 245768 | tf_op jit(solution)/shard_map/ppermute | solution.py:17
  52.5 1.3 collective-permute-start.7
  55.2 1.3 copy.69
  56.5 1.0 copy.47
  57.5 1.6 %collective-permute-done.7 = bf16[1,128,320]{1,2,0:T(8,128)(2,1)} collective-permute-done((bf16[1,128,320]{1,2,0:T(8,128)(2,1)}, bf16[1,128,320]{1,2,0:T(8,128)(2,1)}, u32[]{:S(2)}, u32[]{:S(2)}) %collective-permute-start.7) | collective-permute-done | bytes 81952 | tf_op jit(solution)/shard_map/ppermute | solution.py:19
  59.1 1.3 select_maximum_fusion
  60.5 1.2 fusion.101
  61.7 1.8 %copy.54 = bf16[3,128,320]{2,1,0:T(8,128)(2,1)} copy(bf16[3,128,320]{1,2,0:T(8,128)(2,1)} %get-tuple-element.19) | data formatting | bytes 491520 | tf_op jit(solution)/shard_map/slice | solution.py:101
  63.6 1.7 %pad_maximum_fusion = (bf16[3,128,320]{1,2,0:T(8,128)(2,1)}, bf16[3,128,320]{1,2,0:T(8,128)(2,1)}) fusion(bf16[3,128,320]{1,2,0:T(8,128)(2,1)S(1)} %bitcast_multiply_fusion.2, bf16[1,128,320]{1,2,0:T(8,128)(2,1)} %collective-permute-done.6, bf16[1,128,320]{1,2,0:T(8,128)(2,1)} %collective-permute-done.7), kind=kLoop, calls=%fused_computation.93 | loop fusion | flops 245760 | bytes 901120 | tf_op jit(solution)/shard_map/concatenate | solution.py:15
  65.3 1.9 %copy.55 = bf16[3,128,320]{2,1,0:T(8,128)(2,1)} copy(bf16[3,128,320]{1,2,0:T(8,128)(2,1)} %get-tuple-element.27) | data formatting | bytes 491520 | tf_op jit(solution)/shard_map/slice | solution.py:101
  67.2 1.8 %copy.56 = bf16[3,128,320]{2,1,0:T(8,128)(2,1)} copy(bf16[3,128,320]{1,2,0:T(8,128)(2,1)} %get-tuple-element.18) | data formatting | bytes 491520 | tf_op jit(solution)/shard_map/slice | solution.py:101
  69.0 1.8 %copy.57 = bf16[3,128,320]{2,1,0:T(8,128)(2,1)} copy(bf16[3,128,320]{1,2,0:T(8,128)(2,1)} %get-tuple-element.17) | data formatting | bytes 491520 | tf_op jit(solution)/shard_map/slice | solution.py:101
  70.9 1.8 %copy.59 = bf16[3,128,320]{2,1,0:T(8,128)(2,1)} copy(bf16[3,128,320]{1,2,0:T(8,128)(2,1)} %get-tuple-element.16) | data formatting | bytes 491520 | tf_op jit(solution)/shard_map/slice | solution.py:101
  72.7 0.9 copy.60
  73.6 0.9 copy.61
  74.5 0.9 copy.62
  75.4 1.2 fusion.102
  76.6 1.2 copy.41
  77.8 1.7 %pad_maximum_fusion.2 = (bf16[3,128,320]{1,2,0:T(8,128)(2,1)}, bf16[3,128,320]{1,2,0:T(8,128)(2,1)}) fusion(bf16[1,128,320]{1,2,0:T(8,128)(2,1)} %copy-done.21, bf16[3,128,320]{1,2,0:T(8,128)(2,1)S(1)} %multiply_convert_fusion.4, bf16[1,128,320]{1,2,0:T(8,128)(2,1)} %copy-done.20), kind=kLoop, calls=%fused_computation.95 | loop fusion | flops 245760 | bytes 901120 | tf_op jit(solution)/shard_map/slice | solution.py:78
  79.6 1.9 %copy.43 = bf16[3,128,320]{2,1,0:T(8,128)(2,1)} copy(bf16[3,128,320]{1,2,0:T(8,128)(2,1)} %get-tuple-element.31) | data formatting | bytes 491520 | tf_op jit(solution)/shard_map/slice | solution.py:78
  81.4 0.9 copy.44
  82.4 0.9 copy.45
  83.3 0.9 copy.49
  84.2 0.9 copy.48
  85.3 0.9 copy.51
  86.7 22.2 %all_gather.7 = bf16[4,360,320]{1,2,0:T(8,128)(2,1)S(1)} all-gather(bf16[1,360,320]{1,2,0:T(8,128)(2,1)} %reduce-scatter.2.cloned.1.call-done), channel_id=1, replica_groups=mesh['space'=4,'dp'=8] {'space'}, dimensions={0}, use_global_device_ids=true | all-gather | bytes 1152000 | tf_op jit(solution)/shard_map/all_gather | solution.py:124
  109.3 0.9 copy.70
  110.6 1.0 copy.71
  111.6 4.4 %all-gather.3.cloned.1.call-done = bf16[8,360,320]{1,2,0:T(8,128)(2,1)} async-done(((bf16[1,360,320]{1,2,0:T(8,128)(2,1)}), bf16[8,360,320]{1,2,0:T(8,128)(2,1)}) %all-gather.3.cloned.1.call-update) | async-done | bytes 1843216 | tf_op jit(solution)/shard_map/all_gather | solution.py:62
  116.1 4.0 %copy.42 = bf16[8,360,320]{1,0,2:T(8,128)(2,1)} copy(bf16[8,360,320]{1,2,0:T(8,128)(2,1)} %all-gather.3.cloned.1.call-done) | data formatting | bytes 3686400 | tf_op jit(solution)/shard_map/all_gather | solution.py:62
  120.0 3.4 %reshape.284 = bf16[2880,320]{0,1:T(8,128)(2,1)S(1)} reshape(bf16[8,360,320]{1,0,2:T(8,128)(2,1)} %copy.42) | data formatting | bytes 3686400
  123.8 1.3 fusion.68
  128.7 1.4 fusion.81
  130.1 1.5 convolution_add_fusion.8
  134.7 0.7 fusion.100
  135.6 1.6 %collective-permute-start.8 = (f32[32]{0:T(128)S(1)}, f32[32]{0:T(128)S(1)}, u32[]{:S(2)}, u32[]{:S(2)}) collective-permute-start(f32[32]{0:T(128)S(1)} %reduce_sum.84), channel_id=1, source_target_pairs={{0,8},{8,0},{16,24},{24,16},{1,9},{9,1},{17,25},{25,17},{2,10},{10... | collective-permute-start | bytes 392 | tf_op jit(solution)/shard_map/ppermute | solution.py:33
  138.2 1.0 collective-permute-done.8
  139.2 2.4 %collective-permute-start.9 = (f32[32]{0:T(128)S(1)}, f32[32]{0:T(128)S(1)}, u32[]{:S(2)}, u32[]{:S(2)}) collective-permute-start(f32[32]{0:T(128)S(1)} %add.196), channel_id=1, source_target_pairs={{0,16},{8,24},{16,0},{24,8},{1,17},{9,25},{17,1},{25,9},{2,18},{10... | collective-permute-start | bytes 392 | tf_op jit(solution)/shard_map/ppermute | solution.py:33
  141.7 1.8 %collective-permute-start.11 = (f32[32]{0:T(128)S(1)}, f32[32]{0:T(128)S(1)}, u32[]{:S(2)}, u32[]{:S(2)}) collective-permute-start(f32[32]{0:T(128)S(1)} %add.198), channel_id=1, source_target_pairs={{0,16},{8,24},{16,0},{24,8},{1,17},{9,25},{17,1},{25,9},{2,18},{10... | collective-permute-start | bytes 392 | tf_op jit(solution)/shard_map/ppermute | solution.py:33
  143.7 2.4 %collective-permute-done.11 = f32[32]{0:T(128)S(1)} collective-permute-done((f32[32]{0:T(128)S(1)}, f32[32]{0:T(128)S(1)}, u32[]{:S(2)}, u32[]{:S(2)}) %collective-permute-start.11) | collective-permute-done | bytes 160 | tf_op jit(solution)/shard_map/ppermute | solution.py:33
  146.5 1.3 multiply_convert_fusion.1
  (134 shorter events, 12.9 us)
Async XLA Ops:
  7.2 79.5 %reduce-scatter.2.cloned.1.call-start = ((), (), s32[]{:S(2)}) async-start(), calls=%async_computation.1 | async-start | bytes 2211840 | tf_op jit(solution)/shard_map/reduce_scatter | solution.py:117
  10.0 4.6 %collective-permute-start = (f32[32]{0:T(128)S(1)}, f32[32]{0:T(128)S(1)}, u32[]{:S(2)}, u32[]{:S(2)}) collective-permute-start(f32[32]{0:T(128)S(1)} %reduce_sum.62), channel_id=1, source_target_pairs={{0,8},{8,0},{16,24},{24,16},{1,9},{9,1},{17,25},{25,17},{2,10},{10... | collective-permute-start | bytes 392 | tf_op jit(solution)/shard_map/ppermute | solution.py:33
  13.3 4.3 %collective-permute-start.2 = (f32[32]{0:T(128)S(1)}, f32[32]{0:T(128)S(1)}, u32[]{:S(2)}, u32[]{:S(2)}) collective-permute-start(f32[32]{0:T(128)S(1)} %reduce_sum.81), channel_id=1, source_target_pairs={{0,8},{8,0},{16,24},{24,16},{1,9},{9,1},{17,25},{25,17},{2,10},{10... | collective-permute-start | bytes 392 | tf_op jit(solution)/shard_map/ppermute | solution.py:33
  14.6 4.9 %collective-permute-start.1 = (f32[32]{0:T(128)S(1)}, f32[32]{0:T(128)S(1)}, u32[]{:S(2)}, u32[]{:S(2)}) collective-permute-start(f32[32]{0:T(128)S(1)} %add.161), channel_id=1, source_target_pairs={{0,16},{8,24},{16,0},{24,8},{1,17},{9,25},{17,1},{25,9},{2,18},{10... | collective-permute-start | bytes 392 | tf_op jit(solution)/shard_map/ppermute | solution.py:33
  17.6 4.4 %collective-permute-start.3 = (f32[32]{0:T(128)S(1)}, f32[32]{0:T(128)S(1)}, u32[]{:S(2)}, u32[]{:S(2)}) collective-permute-start(f32[32]{0:T(128)S(1)} %add.163), channel_id=1, source_target_pairs={{0,16},{8,24},{16,0},{24,8},{1,17},{9,25},{17,1},{25,9},{2,18},{10... | collective-permute-start | bytes 392 | tf_op jit(solution)/shard_map/ppermute | solution.py:33
  22.5 15.7 %copy-start.23 = (f32[320]{0:T(512)}, f32[320]{0:T(512)S(1)}, u32[]{:S(2)}) copy-start(f32[320]{0:T(512)S(1)} %sub.55) | copy-start | bytes 3844
  23.8 5.8 %collective-permute-start.4 = (bf16[1,128,320]{1,2,0:T(8,128)(2,1)S(1)}, bf16[1,128,320]{1,2,0:T(8,128)(2,1)S(1)}, u32[]{:S(2)}, u32[]{:S(2)}) collective-permute-start(bf16[1,128,320]{1,2,0:T(8,128)(2,1)S(1)} %get-tuple-element.32), channel_id=1, source_target_pairs={{0,8},{8,16},{16,24},{1,9},{9,17},{17,25},{2,10},{10,18},{18,26},{... | collective-permute-start | bytes 245768 | tf_op jit(solution)/shard_map/ppermute | solution.py:17
  27.2 6.3 %collective-permute-start.5 = (bf16[1,128,320]{1,2,0:T(8,128)(2,1)S(1)}, bf16[1,128,320]{1,2,0:T(8,128)(2,1)S(1)}, u32[]{:S(2)}, u32[]{:S(2)}) collective-permute-start(bf16[1,128,320]{1,2,0:T(8,128)(2,1)S(1)} %get-tuple-element.33), channel_id=1, source_target_pairs={{8,0},{16,8},{24,16},{9,1},{17,9},{25,17},{10,2},{18,10},{26,18},{... | collective-permute-start | bytes 245768 | tf_op jit(solution)/shard_map/ppermute | solution.py:19
  29.5 7.6 %copy-start.20 = (bf16[1,128,320]{1,2,0:T(8,128)(2,1)}, bf16[1,128,320]{1,2,0:T(8,128)(2,1)S(1)}, u32[]{:S(2)}) copy-start(bf16[1,128,320]{1,2,0:T(8,128)(2,1)S(1)} %collective-permute-done.4) | copy-start | bytes 245764
  33.6 7.9 %copy-start.21 = (bf16[1,128,320]{1,2,0:T(8,128)(2,1)}, bf16[1,128,320]{1,2,0:T(8,128)(2,1)S(1)}, u32[]{:S(2)}) copy-start(bf16[1,128,320]{1,2,0:T(8,128)(2,1)S(1)} %collective-permute-done.5) | copy-start | bytes 245764
  34.0 4.2 %copy-start = (bf16[1,3,128,320]{2,3,1,0:T(8,128)(2,1)S(1)}, bf16[1,3,128,320]{2,3,1,0:T(8,128)(2,1)}, u32[]{:S(2)}) copy-start(bf16[1,3,128,320]{2,3,1,0:T(8,128)(2,1)} %param.9) | copy-start | bytes 737284
  34.0 4.2 %copy-start.11 = (bf16[1,3,128,320]{2,3,1,0:T(8,128)(2,1)S(1)}, bf16[1,3,128,320]{2,3,1,0:T(8,128)(2,1)}, u32[]{:S(2)}) copy-start(bf16[1,3,128,320]{2,3,1,0:T(8,128)(2,1)} %param.10) | copy-start | bytes 737284
  34.0 4.2 %copy-start.26 = (f32[320]{0:T(512)S(1)}, f32[320]{0:T(512)}, u32[]{:S(2)}) copy-start(f32[320]{0:T(512)} %param.12) | copy-start | bytes 3844
  34.0 4.2 %copy-start.29 = (f32[320]{0:T(512)S(1)}, f32[320]{0:T(512)}, u32[]{:S(2)}) copy-start(f32[320]{0:T(512)} %param.11) | copy-start | bytes 3844
  47.7 7.3 %copy-start.17 = (f32[360,320]{0,1:T(8,128)S(1)}, f32[360,320]{0,1:T(8,128)}, u32[]{:S(2)}) copy-start(f32[360,320]{0,1:T(8,128)} %param.14) | copy-start | bytes 1382404
  47.7 68.4 %all-gather.3.cloned.1.call-start = ((), (), s32[]{:S(2)}) async-start(), calls=%async_computation.2 | async-start | bytes 2211840 | tf_op jit(solution)/shard_map/all_gather | solution.py:62
  49.1 8.4 %collective-permute-start.6 = (bf16[1,128,320]{1,2,0:T(8,128)(2,1)}, bf16[1,128,320]{1,2,0:T(8,128)(2,1)}, u32[]{:S(2)}, u32[]{:S(2)}) collective-permute-start(bf16[1,128,320]{1,2,0:T(8,128)(2,1)} %get-tuple-element.28), channel_id=1, source_target_pairs={{0,8},{8,16},{16,24},{1,9},{9,17},{17,25},{2,10},{10,18},{18,26},{... | collective-permute-start | bytes 245768 | tf_op jit(solution)/shard_map/ppermute | solution.py:17
  52.5 6.6 %collective-permute-start.7 = (bf16[1,128,320]{1,2,0:T(8,128)(2,1)}, bf16[1,128,320]{1,2,0:T(8,128)(2,1)}, u32[]{:S(2)}, u32[]{:S(2)}) collective-permute-start(bf16[1,128,320]{1,2,0:T(8,128)(2,1)} %get-tuple-element.29), channel_id=1, source_target_pairs={{8,0},{16,8},{24,16},{9,1},{17,9},{25,17},{10,2},{18,10},{26,18},{... | collective-permute-start | bytes 245768 | tf_op jit(solution)/shard_map/ppermute | solution.py:19
  65.3 8.3 %copy-start.15 = (bf16[3,128,320]{1,2,0:T(8,128)(2,1)S(1)}, bf16[3,128,320]{1,2,0:T(8,128)(2,1)}, u32[]{:S(2)}) copy-start(bf16[3,128,320]{1,2,0:T(8,128)(2,1)} %get-tuple-element.26) | copy-start | bytes 737284
  76.6 4.8 %copy-start.14 = (bf16[3,128,320]{1,2,0:T(8,128)(2,1)S(1)}, bf16[3,128,320]{1,2,0:T(8,128)(2,1)}, u32[]{:S(2)}) copy-start(bf16[3,128,320]{1,2,0:T(8,128)(2,1)} %get-tuple-element.24) | copy-start | bytes 737284
  76.6 5.8 %copy-start.13 = (bf16[3,128,320]{1,2,0:T(8,128)(2,1)S(1)}, bf16[3,128,320]{1,2,0:T(8,128)(2,1)}, u32[]{:S(2)}) copy-start(bf16[3,128,320]{1,2,0:T(8,128)(2,1)} %get-tuple-element.23) | copy-start | bytes 737284
  76.6 6.7 %copy-start.12 = (bf16[3,128,320]{1,2,0:T(8,128)(2,1)S(1)}, bf16[3,128,320]{1,2,0:T(8,128)(2,1)}, u32[]{:S(2)}) copy-start(bf16[3,128,320]{1,2,0:T(8,128)(2,1)} %get-tuple-element.21) | copy-start | bytes 737284
  79.6 5.6 %copy-start.16 = (bf16[3,128,320]{1,2,0:T(8,128)(2,1)S(1)}, bf16[3,128,320]{1,2,0:T(8,128)(2,1)}, u32[]{:S(2)}) copy-start(bf16[3,128,320]{1,2,0:T(8,128)(2,1)} %get-tuple-element.30) | copy-start | bytes 737284
  123.4 1.7 %copy-start.10 = (bf16[3,128,320]{2,1,0:T(8,128)(2,1)S(1)}, bf16[3,128,320]{2,1,0:T(8,128)(2,1)}, u32[]{:S(2)}) copy-start(bf16[3,128,320]{2,1,0:T(8,128)(2,1)} %copy.48) | copy-start | bytes 737284
  123.4 2.1 %copy-start.9 = (bf16[3,128,320]{2,1,0:T(8,128)(2,1)S(1)}, bf16[3,128,320]{2,1,0:T(8,128)(2,1)}, u32[]{:S(2)}) copy-start(bf16[3,128,320]{2,1,0:T(8,128)(2,1)} %copy.43) | copy-start | bytes 737284
  123.8 2.2 %copy-start.8 = (bf16[3,128,320]{2,1,0:T(8,128)(2,1)S(1)}, bf16[3,128,320]{2,1,0:T(8,128)(2,1)}, u32[]{:S(2)}) copy-start(bf16[3,128,320]{2,1,0:T(8,128)(2,1)} %copy.44) | copy-start | bytes 737284
  125.1 1.2 copy-start.7
  125.9 1.1 copy-start.18
  125.9 1.0 copy-start.24
  125.9 1.0 copy-start.27
  125.9 1.0 copy-start.30
  125.9 1.0 copy-start.33
  127.0 1.0 copy-start.6
  128.7 2.9 %copy-start.5 = (bf16[3,128,320]{2,1,0:T(8,128)(2,1)S(1)}, bf16[3,128,320]{2,1,0:T(8,128)(2,1)}, u32[]{:S(2)}) copy-start(bf16[3,128,320]{2,1,0:T(8,128)(2,1)} %copy.56) | copy-start | bytes 737284
  128.7 3.3 %copy-start.4 = (bf16[3,128,320]{2,1,0:T(8,128)(2,1)S(1)}, bf16[3,128,320]{2,1,0:T(8,128)(2,1)}, u32[]{:S(2)}) copy-start(bf16[3,128,320]{2,1,0:T(8,128)(2,1)} %copy.57) | copy-start | bytes 737284
  132.0 1.0 copy-start.3
  132.6 1.0 copy-start.1
  133.0 1.0 copy-start.2
  133.5 1.1 copy-start.19
  133.5 1.1 copy-start.22
  133.6 1.1 copy-start.25
  133.6 1.1 copy-start.28
  133.6 1.1 copy-start.31
  133.6 1.1 copy-start.32
  135.6 3.6 %collective-permute-start.8 = (f32[32]{0:T(128)S(1)}, f32[32]{0:T(128)S(1)}, u32[]{:S(2)}, u32[]{:S(2)}) collective-permute-start(f32[32]{0:T(128)S(1)} %reduce_sum.84), channel_id=1, source_target_pairs={{0,8},{8,0},{16,24},{24,16},{1,9},{9,1},{17,25},{25,17},{2,10},{10... | collective-permute-start | bytes 392 | tf_op jit(solution)/shard_map/ppermute | solution.py:33
  137.4 4.3 %collective-permute-start.10 = (f32[32]{0:T(128)S(1)}, f32[32]{0:T(128)S(1)}, u32[]{:S(2)}, u32[]{:S(2)}) collective-permute-start(f32[32]{0:T(128)S(1)} %reduce_sum.87), channel_id=1, source_target_pairs={{0,8},{8,0},{16,24},{24,16},{1,9},{9,1},{17,25},{25,17},{2,10},{10... | collective-permute-start | bytes 392 | tf_op jit(solution)/shard_map/ppermute | solution.py:33
  139.2 4.4 %collective-permute-start.9 = (f32[32]{0:T(128)S(1)}, f32[32]{0:T(128)S(1)}, u32[]{:S(2)}, u32[]{:S(2)}) collective-permute-start(f32[32]{0:T(128)S(1)} %add.196), channel_id=1, source_target_pairs={{0,16},{8,24},{16,0},{24,8},{1,17},{9,25},{17,1},{25,9},{2,18},{10... | collective-permute-start | bytes 392 | tf_op jit(solution)/shard_map/ppermute | solution.py:33
  141.7 4.4 %collective-permute-start.11 = (f32[32]{0:T(128)S(1)}, f32[32]{0:T(128)S(1)}, u32[]{:S(2)}, u32[]{:S(2)}) collective-permute-start(f32[32]{0:T(128)S(1)} %add.198), channel_id=1, source_target_pairs={{0,16},{8,24},{16,0},{24,8},{1,17},{9,25},{17,1},{25,9},{2,18},{10... | collective-permute-start | bytes 392 | tf_op jit(solution)/shard_map/ppermute | solution.py:33
Sparse Core Ops, SparseCore 0:
  47.8 38.7 reduce-scatter.1
  88.7 27.3 all-gather.2
